TPU v7x, 512 devices: a whole 4x8x8 slice. The times are simulated.
512 devices in a mesh: depth: 16 (over x_hi, y), scan: 32 (over z, x_lo, core).
Axes of the slice: x: 4 (x_hi: 2, x_lo: 2; x = x_hi * 2 + x_lo), y: 8, z: 8, core: 2. Of those that a mesh axis runs over, the one named last changes fastest.
Arguments:
- object_slice: bfloat16 [2, 4, 512, 2048], P(None, None, 'depth', 'scan'), may hold values from -4 to 4
- probe_field: bfloat16 [2, 512, 512], replicated, may hold values from -2 to 2
- offsets: int32 [64, 2], replicated, may hold values from 0 to 1536
- assignment: int32 [64], P('scan'), may hold values from 0 to 63, each once
- intensities: float32 [64, 512, 512], P('scan', 'depth'), may hold values from 0 to 3
Outputs:
- object_grad: float32 [2, 4, 512, 2048], P(None, None, 'depth', 'scan')
- probe_grad: float32 [2, 512, 512], P(None, 'depth')
Inputs may be any that keep to these rules, and one draw needn't show every extreme that they name: `offsets`: each window lies inside the object window. `assignment`: every position stands in exactly one slot; slots s * 2 to s * 2 + 1 lie on index s of scan.
All inputs are finite; a program needn't handle non-finite values.
Results may differ from a plain program's by a relative error of at most 0.0003.
Values may be sent and summed in bfloat16 or wider, within the bound.
No kernel may reach another device: no remote copies, remote signals or barrier semaphores. Data moves between devices by JAX's collectives and lax.ppermute only.
A program may use at most 64 MiB of HBM per device.

v0:
```python
import math
import jax
import jax.numpy as jnp
from jax import lax
from jax.sharding import PartitionSpec as P

fresnel_scale = 4


def from_behind(block, axis, distance):
    devices = range(lax.axis_size(axis))
    route = [((i - distance) % len(devices), i) for i in devices]
    return lax.ppermute(block, axis, route)


def dft_table(size):
    index = jnp.arange(size, dtype=jnp.int32)
    turns = index[:, None] * index[None, :] % size
    angle = 2.0 * math.pi / size * turns.astype(jnp.float32)
    norm = 1.0 / math.sqrt(size)
    return (jnp.cos(angle) * norm, -jnp.sin(angle) * norm)


def chirp_phase(index, size):
    centred = index - size // 2
    period = 2 * fresnel_scale * size
    phase = centred * centred % period
    angle = math.pi / (fresnel_scale * size) * phase.astype(jnp.float32)
    return (jnp.cos(angle), jnp.sin(angle))


def contract(form, left_side, right_side):
    return jnp.einsum(
        form,
        left_side,
        right_side,
        precision=lax.Precision.HIGHEST,
        preferred_element_type=jnp.float32,
    )


def complex_mix(form, left_re, left_im, right_re, right_im):
    real_part = contract(form, left_re, right_re) - contract(form, left_im, right_im)
    imag_part = contract(form, left_re, right_im) + contract(form, left_im, right_re)
    return (real_part, imag_part)


def on_device(object_slice, probe_field, offsets, assignment, intensities):
    depth_count = lax.axis_size("depth")
    depth_index = lax.axis_index("depth")
    rows_dev = object_slice.shape[2]
    cycles = object_slice.shape[1]
    patch_side = probe_field.shape[2]
    pos_count = assignment.shape[0]
    total_pos = pos_count * lax.axis_size("scan")
    band_rows = lax.all_gather(object_slice, "scan", axis=3, tiled=True)
    full_width = band_rows.shape[3]
    flat_band = band_rows.reshape(2, cycles * rows_dev, full_width)
    position = offsets[assignment]
    top_row = position[:, 0]
    left_col = position[:, 1]
    table_re, table_im = dft_table(patch_side)
    row_ids = jnp.arange(rows_dev, dtype=jnp.int32)
    col_ids = jnp.arange(patch_side, dtype=jnp.int32)
    col_cos, col_sin = chirp_phase(col_ids, patch_side)
    zero_start = jnp.int32(0)

    def cut_tile(cycle_row, column):
        return lax.dynamic_slice(
            flat_band, (zero_start, cycle_row * rows_dev, column), (2, rows_dev, patch_side)
        )

    block_first = top_row // rows_dev
    offset_in = top_row % rows_dev
    first_block = block_first + (depth_index - block_first) % depth_count
    first_cycle = first_block // depth_count
    second_cycle = jnp.minimum(first_cycle + 1, cycles - 1)
    pair_tiles = jnp.stack(
        [jax.vmap(cut_tile)(first_cycle, left_col), jax.vmap(cut_tile)(second_cycle, left_col)], 1
    )
    levels = depth_count.bit_length() - 1
    amount = (depth_count - block_first % depth_count) % depth_count
    for level in range(levels):
        moved = from_behind(pair_tiles, "depth", 1 << level)
        taken = amount >> level & 1 == 1
        pair_tiles = jnp.where(taken[:, None, None, None, None], moved, pair_tiles)
    first_tile = pair_tiles[:, 0]
    outgoing = jnp.where(depth_index == 0, pair_tiles[:, 1], first_tile)
    following = from_behind(outgoing, "depth", depth_count - 1)
    stacked = jnp.concatenate([first_tile, following], 2)

    def take_rows(tile_pair, corner_row):
        return lax.dynamic_slice_in_dim(tile_pair, corner_row, rows_dev, 1)

    patch = jax.vmap(take_rows)(stacked, offset_in)
    patch_rows = jnp.broadcast_to(depth_index * rows_dev + row_ids[None, :], (pos_count, rows_dev))
    probe_rows = lax.dynamic_slice_in_dim(probe_field, depth_index * rows_dev, rows_dev, 1)[None]
    row_cos, row_sin = chirp_phase(patch_rows, patch_side)
    chirp_re = (
        row_cos[:, :, None] * col_cos[None, None, :] - row_sin[:, :, None] * col_sin[None, None, :]
    )
    chirp_im = (
        row_sin[:, :, None] * col_cos[None, None, :] + row_cos[:, :, None] * col_sin[None, None, :]
    )
    obj_re = patch[:, 0].astype(jnp.float32)
    obj_im = patch[:, 1].astype(jnp.float32)
    probe_re = probe_rows[:, 0].astype(jnp.float32)
    probe_im = probe_rows[:, 1].astype(jnp.float32)
    wave_re = probe_re * obj_re - probe_im * obj_im
    wave_im = probe_re * obj_im + probe_im * obj_re
    psi_re = wave_re * chirp_re - wave_im * chirp_im
    psi_im = wave_re * chirp_im + wave_im * chirp_re
    half_re, half_im = complex_mix("vk,pjk->pvj", table_re, table_im, psi_re, psi_im)
    half_re, half_im = (
        lax.all_to_all(half_re, "depth", split_axis=1, concat_axis=2, tiled=True),
        lax.all_to_all(half_im, "depth", split_axis=1, concat_axis=2, tiled=True),
    )
    far_re, far_im = complex_mix("pvj,ju->pvu", half_re, half_im, table_re, table_im)
    excess = far_re * far_re + far_im * far_im - intensities
    resid_re = excess * far_re
    resid_im = excess * far_im
    mid_re, mid_im = complex_mix("pvu,uj->pvj", resid_re, resid_im, table_re, -table_im)
    mid_re, mid_im = (
        lax.all_to_all(mid_re, "depth", split_axis=2, concat_axis=1, tiled=True),
        lax.all_to_all(mid_im, "depth", split_axis=2, concat_axis=1, tiled=True),
    )
    back_re, back_im = complex_mix("vk,pvj->pjk", table_re, -table_im, mid_re, mid_im)
    grad_re = back_re * chirp_re + back_im * chirp_im
    grad_im = back_im * chirp_re - back_re * chirp_im
    contrib = jnp.stack(
        [probe_re * grad_re + probe_im * grad_im, probe_re * grad_im - probe_im * grad_re], 1
    )
    term_re = obj_re * grad_re + obj_im * grad_im
    term_im = obj_re * grad_im - obj_im * grad_re
    grad_band = jnp.zeros((2, cycles * rows_dev, full_width), jnp.float32)

    def add_tile(band_now, tile_value, cycle_row, column):
        corner = (zero_start, cycle_row * rows_dev, column)
        current = lax.dynamic_slice(band_now, corner, (2, rows_dev, patch_side))
        return lax.dynamic_update_slice(band_now, current + tile_value, corner)

    empty_window = jnp.zeros((pos_count, 2, 2 * rows_dev, patch_side), jnp.float32)

    def place_rows(window_zero, tile_rows, corner_row):
        return lax.dynamic_update_slice_in_dim(window_zero, tile_rows, corner_row, 1)

    placed = jax.vmap(place_rows)(empty_window, contrib, offset_in)
    head_part = placed[:, :, :rows_dev]
    tail_part = placed[:, :, rows_dev:]
    returned = from_behind(tail_part, "depth", 1)
    is_first = depth_index == 0
    head_part = jnp.where(is_first, head_part, head_part + returned)
    second_part = jnp.where(is_first, returned, jnp.zeros_like(returned))
    grad_pair = jnp.stack([head_part, second_part], 1)
    amount_back = block_first % depth_count
    for level in range(levels):
        moved_back = from_behind(grad_pair, "depth", 1 << level)
        taken_back = amount_back >> level & 1 == 1
        grad_pair = jnp.where(taken_back[:, None, None, None, None], moved_back, grad_pair)
    for slot_index in range(pos_count):
        grad_band = add_tile(
            grad_band, grad_pair[slot_index, 0], first_cycle[slot_index], left_col[slot_index]
        )
        grad_band = add_tile(
            grad_band, grad_pair[slot_index, 1], second_cycle[slot_index], left_col[slot_index]
        )
    probe_sum = jnp.stack([jnp.sum(term_re, 0), jnp.sum(term_im, 0)])
    probe_grad = lax.psum(probe_sum, "scan")
    object_grad = lax.psum_scatter(
        grad_band.reshape(2, cycles, rows_dev, full_width), "scan", scatter_dimension=3, tiled=True
    )
    return (object_grad, probe_grad * total_pos ** (-0.5))


def solution(mesh):
    return jax.shard_map(
        on_device,
        mesh=mesh,
        in_specs=(P(None, None, "depth", "scan"), P(), P(), P("scan"), P("scan", "depth", None)),
        out_specs=(P(None, None, "depth", "scan"), P(None, "depth", None)),
        check_vma=False,
    )
```

profile of v0, /device:TPU:8, one launch (start us, length us, event | category | flops | bytes accessed | tf_op | source)
XLA Modules:
  0.0 748.6 jit_solution(7698439106445803496)
XLA Ops:
  7.2 1.7 copy.63
  11.9 73.0 %all-gather.2.cloned.1.call-done = bf16[2,4,32,2048]{2,1,0,3:T(4,128)(2,1)} async-done(((bf16[2,4,32,64]{2,1,0,3:T(4,128)(2,1)}), bf16[2,4,32,2048]{2,1,0,3:T(4,128)(2,1)}) %all-gather.2.cloned.1.call-update) | async-done | bytes 1048592 | tf_op jit(solution)/shard_map/all_gather | solution.py:56
  85.0 5.5 copy.64
  90.5 4.2 while.4
  91.2 1.4 dynamic-slice_bitcast_fusion.6
  93.3 1.4 dynamic-slice_bitcast_fusion.6
  94.8 4.2 while.3
  95.4 1.4 dynamic-slice_bitcast_fusion.5
  97.5 1.4 dynamic-slice_bitcast_fusion.5
  99.4 3.4 collective-permute-start
  102.9 6.9 collective-permute-done
  110.3 4.5 collective-permute-start.1
  114.8 9.8 %collective-permute-done.1 = bf16[2,2,2,32,512]{4,2,0,3,1:T(2,128)(2,1)S(1)} collective-permute-done((bf16[2,2,2,32,512]{4,2,0,3,1:T(2,128)(2,1)S(1)}, bf16[2,2,2,32,512]{4,2,0,3,1:T(2,128)(2,1)S(1)}, u32[]{:S(2)}, u32[]{:S(2)}) %collective-permute-start.1) | collective-permute-done | bytes 262176 | tf_op jit(solution)/shard_map/ppermute | solution.py:13
  125.3 4.8 collective-permute-start.2
  130.1 15.7 %collective-permute-done.2 = bf16[2,2,2,32,512]{4,2,0,3,1:T(2,128)(2,1)S(1)} collective-permute-done((bf16[2,2,2,32,512]{4,2,0,3,1:T(2,128)(2,1)S(1)}, bf16[2,2,2,32,512]{4,2,0,3,1:T(2,128)(2,1)S(1)}, u32[]{:S(2)}, u32[]{:S(2)}) %collective-permute-start.2) | collective-permute-done | bytes 262176 | tf_op jit(solution)/shard_map/ppermute | solution.py:13
  146.2 2.8 collective-permute-start.3
  149.0 8.0 %collective-permute-done.3 = bf16[2,2,2,32,512]{4,2,0,3,1:T(2,128)(2,1)S(1)} collective-permute-done((bf16[2,2,2,32,512]{4,2,0,3,1:T(2,128)(2,1)S(1)}, bf16[2,2,2,32,512]{4,2,0,3,1:T(2,128)(2,1)S(1)}, u32[]{:S(2)}, u32[]{:S(2)}) %collective-permute-start.3) | collective-permute-done | bytes 262176 | tf_op jit(solution)/shard_map/ppermute | solution.py:13
  157.6 8.7 %collective-permute-start.4 = (bf16[2,2,32,512]{3,1,0,2:T(2,128)(2,1)S(1)}, bf16[2,2,32,512]{3,1,0,2:T(2,128)(2,1)S(1)}, u32[]{:S(2)}, u32[]{:S(2)}) collective-permute-start(bf16[2,2,32,512]{3,1,0,2:T(2,128)(2,1)S(1)} %broadcast_select_fusion.8), channel_id=1, source_target_pairs={{32,0},{64,32},{96,64},{128,96},{160,128},{192,160},{224,192},{256... | collective-permute-start | bytes 393224 | tf_op jit(solution)/shard_map/ppermute | solution.py:13
  166.4 2.2 collective-permute-done.4
  170.0 5.0 fusion.27
  175.0 5.0 fusion.23
  180.0 5.2 fusion.1
  186.7 7.4 all-to-all-start
  194.0 5.0 fusion
  200.5 3.1 all-to-all-done
  203.5 7.1 all-to-all-start.1
  213.1 4.8 fusion.25
  217.8 4.8 fusion.10
  224.6 4.7 convolution_add_fusion.2
  229.3 4.9 convolution_subtract_fusion.2
  234.3 4.8 fusion.7
  239.1 4.8 fusion.20
  243.9 4.8 convolution_subtract_fusion.1
  250.2 9.6 %all-to-all-start.2 = ((f32[16,1,2048]{2,1,0:T(1,128)}), f32[16,1,2048]{2,1,0:T(1,128)S(1)}, u32[]{:S(2)}, u32[]{:S(2)}) async-start(f32[16,1,2048]{2,1,0:T(1,128)} %reshape.375), calls=%async_computation.2 | async-start | bytes 262144 | tf_op jit(solution)/shard_map/all_to_all | solution.py:124
  259.8 4.7 convolution_add_fusion.1
  266.0 3.3 all-to-all-done.2
  269.3 6.3 all-to-all-start.3
  277.7 5.0 fusion.18
  282.7 2.5 all-to-all-done.3
  287.1 4.8 fusion.15
  291.9 4.8 convolution_add_fusion
  296.7 4.9 fusion.40
  301.8 14.5 %while.5 = (s32[]{:T(128)}, f32[2,2,64,512]{3,1,0,2:T(2,128)S(1)}, s32[2,4]{1,0:T(2,128)S(1)}, f32[2,2,32,512]{3,2,0,1:T(8,128)S(1)}, s32[]{:T(128)}, /*index=5*/s32[4]{0:T(128)S(1)}) while((s32[]{:T(128)}, f32[2,2,64,512]{3,1,0,2:T(2,128)S(1)}, s32[2,4]{1,0:T(2,128)S(1)}, f32[2,2,32,512]{3,2,0,1:T(8,128)S(1)}, s32[]{:T(128)}, ...), condition=%wide.while_cond.2, body=%wide.while_body.2.sunk | while | flops 32797 | bytes 917703 | solution.py:145
  302.5 3.2 and_reduce_fusion.2
  309.7 3.2 and_reduce_fusion.2
  316.3 2.6 collective-permute-start.5
  318.9 5.6 collective-permute-done.5
  325.0 4.3 collective-permute-start.6
  329.3 9.1 %collective-permute-done.6 = f32[2,2,2,32,512]{4,2,0,3,1:T(2,128)S(1)} collective-permute-done((f32[2,2,2,32,512]{4,2,0,3,1:T(2,128)S(1)}, f32[2,2,2,32,512]{4,2,0,3,1:T(2,128)S(1)}, u32[]{:S(2)}, u32[]{:S(2)}) %collective-permute-start.6) | collective-permute-done | bytes 524320 | tf_op jit(solution)/shard_map/ppermute | solution.py:13
  338.8 4.0 collective-permute-start.7
  342.8 18.4 %collective-permute-done.7 = f32[2,2,2,32,512]{4,2,0,3,1:T(2,128)S(1)} collective-permute-done((f32[2,2,2,32,512]{4,2,0,3,1:T(2,128)S(1)}, f32[2,2,2,32,512]{4,2,0,3,1:T(2,128)S(1)}, u32[]{:S(2)}, u32[]{:S(2)}) %collective-permute-start.7) | collective-permute-done | bytes 524320 | tf_op jit(solution)/shard_map/ppermute | solution.py:13
  361.6 4.7 collective-permute-start.8
  366.3 20.3 %collective-permute-done.8 = f32[2,2,2,32,512]{4,2,0,3,1:T(2,128)S(1)} collective-permute-done((f32[2,2,2,32,512]{4,2,0,3,1:T(2,128)S(1)}, f32[2,2,2,32,512]{4,2,0,3,1:T(2,128)S(1)}, u32[]{:S(2)}, u32[]{:S(2)}) %collective-permute-start.8) | collective-permute-done | bytes 524320 | tf_op jit(solution)/shard_map/ppermute | solution.py:13
  387.0 1.9 collective-permute-start.9
  397.3 2.3 collective-permute-done.9
  401.8 6.2 dynamic_update_slice.12
  409.1 6.2 dynamic_update_slice.13
  416.4 6.1 dynamic_update_slice.14
  423.7 6.1 dynamic_update_slice.15
  429.8 6.1 copy.84
  436.0 8.6 %reshape.365 = f32[2048,256]{1,0:T(8,128)} reshape(f32[2048,2,4,32]{3,2,1,0:T(4,128)} %bitcast.195) | data formatting | bytes 4194304
  444.6 169.5 %all-reduce.2.cloned.1.call-done = f32[2,32,512]{2,1,0:T(8,128)} async-done(((f32[2,32,512]{2,1,0:T(8,128)}), f32[2,32,512]{2,1,0:T(8,128)}) %all-reduce.2.cloned.1.call-update) | async-done | bytes 131088 | tf_op jit(solution)/shard_map/psum | solution.py:168
  614.0 1.6 broadcast_multiply_fusion
  615.6 124.2 %reduce-scatter.4.cloned.1.call-done = f32[64,256]{1,0:T(8,128)} async-done(((f32[2048,256]{1,0:T(8,128)}), f32[64,256]{1,0:T(8,128)}) %reduce-scatter.4.cloned.1.call-update) | async-done | bytes 65552
  (115 shorter events, 42.9 us)
Async XLA Ops:
  7.2 107.7 %copy-start = (bf16[2,512,512]{2,1,0:T(8,128)(2,1)S(1)}, bf16[2,512,512]{2,1,0:T(8,128)(2,1)}, u32[]{:S(2)}) copy-start(bf16[2,512,512]{2,1,0:T(8,128)(2,1)} %param.6) | copy-start | bytes 3145732
  7.2 77.8 %all-gather.2.cloned.1.call-start = ((), (), s32[]{:S(2)}) async-start(), calls=%async_computation.5 | async-start | bytes 4325376 | tf_op jit(solution)/shard_map/all_gather | solution.py:56
  99.4 10.3 %collective-permute-start = (bf16[2,2,2,32,512]{4,2,0,3,1:T(2,128)(2,1)S(1)}, bf16[2,2,2,32,512]{4,2,0,3,1:T(2,128)(2,1)S(1)}, u32[]{:S(2)}, u32[]{:S(2)}) collective-permute-start(bf16[2,2,2,32,512]{4,2,0,3,1:T(2,128)(2,1)S(1)} %pad_maximum_fusion.1), channel_id=1, source_target_pairs={{480,0},{0,32},{32,64},{64,96},{96,128},{128,160},{160,192},{192,2... | collective-permute-start | bytes 786440 | tf_op jit(solution)/shard_map/ppermute | solution.py:13
  110.3 14.4 %collective-permute-start.1 = (bf16[2,2,2,32,512]{4,2,0,3,1:T(2,128)(2,1)S(1)}, bf16[2,2,2,32,512]{4,2,0,3,1:T(2,128)(2,1)S(1)}, u32[]{:S(2)}, u32[]{:S(2)}) collective-permute-start(bf16[2,2,2,32,512]{4,2,0,3,1:T(2,128)(2,1)S(1)} %broadcast_select_fusion.4), channel_id=1, source_target_pairs={{448,0},{480,32},{0,64},{32,96},{64,128},{96,160},{128,192},{160,2... | collective-permute-start | bytes 786440 | tf_op jit(solution)/shard_map/ppermute | solution.py:13
  125.3 20.5 %collective-permute-start.2 = (bf16[2,2,2,32,512]{4,2,0,3,1:T(2,128)(2,1)S(1)}, bf16[2,2,2,32,512]{4,2,0,3,1:T(2,128)(2,1)S(1)}, u32[]{:S(2)}, u32[]{:S(2)}) collective-permute-start(bf16[2,2,2,32,512]{4,2,0,3,1:T(2,128)(2,1)S(1)} %broadcast_select_fusion.5), channel_id=1, source_target_pairs={{384,0},{416,32},{448,64},{480,96},{0,128},{32,160},{64,192},{96,2... | collective-permute-start | bytes 786440 | tf_op jit(solution)/shard_map/ppermute | solution.py:13
  146.2 10.9 %collective-permute-start.3 = (bf16[2,2,2,32,512]{4,2,0,3,1:T(2,128)(2,1)S(1)}, bf16[2,2,2,32,512]{4,2,0,3,1:T(2,128)(2,1)S(1)}, u32[]{:S(2)}, u32[]{:S(2)}) collective-permute-start(bf16[2,2,2,32,512]{4,2,0,3,1:T(2,128)(2,1)S(1)} %broadcast_select_fusion.6), channel_id=1, source_target_pairs={{256,0},{288,32},{320,64},{352,96},{384,128},{416,160},{448,192},{... | collective-permute-start | bytes 786440 | tf_op jit(solution)/shard_map/ppermute | solution.py:13
  157.6 11.0 %collective-permute-start.4 = (bf16[2,2,32,512]{3,1,0,2:T(2,128)(2,1)S(1)}, bf16[2,2,32,512]{3,1,0,2:T(2,128)(2,1)S(1)}, u32[]{:S(2)}, u32[]{:S(2)}) collective-permute-start(bf16[2,2,32,512]{3,1,0,2:T(2,128)(2,1)S(1)} %broadcast_select_fusion.8), channel_id=1, source_target_pairs={{32,0},{64,32},{96,64},{128,96},{160,128},{192,160},{224,192},{256... | collective-permute-start | bytes 393224 | tf_op jit(solution)/shard_map/ppermute | solution.py:13
  186.7 16.9 %all-to-all-start = ((f32[16,1,2048]{2,1,0:T(1,128)}), f32[16,1,2048]{2,1,0:T(1,128)S(1)}, u32[]{:S(2)}, u32[]{:S(2)}) async-start(f32[16,1,2048]{2,1,0:T(1,128)} %reshape.369), calls=%async_computation | async-start | bytes 262144 | tf_op jit(solution)/shard_map/all_to_all | solution.py:115
  203.5 19.1 %all-to-all-start.1 = ((f32[16,1,2048]{2,1,0:T(1,128)}), f32[16,1,2048]{2,1,0:T(1,128)S(1)}, u32[]{:S(2)}, u32[]{:S(2)}) async-start(f32[16,1,2048]{2,1,0:T(1,128)} %reshape.371), calls=%async_computation.1 | async-start | bytes 262144 | tf_op jit(solution)/shard_map/all_to_all | solution.py:116
  229.3 5.0 copy-start.3
  250.2 19.1 %all-to-all-start.2 = ((f32[16,1,2048]{2,1,0:T(1,128)}), f32[16,1,2048]{2,1,0:T(1,128)S(1)}, u32[]{:S(2)}, u32[]{:S(2)}) async-start(f32[16,1,2048]{2,1,0:T(1,128)} %reshape.375), calls=%async_computation.2 | async-start | bytes 262144 | tf_op jit(solution)/shard_map/all_to_all | solution.py:124
  269.3 15.8 %all-to-all-start.3 = ((f32[16,1,2048]{2,1,0:T(1,128)}), f32[16,1,2048]{2,1,0:T(1,128)S(1)}, u32[]{:S(2)}, u32[]{:S(2)}) async-start(f32[16,1,2048]{2,1,0:T(1,128)} %reshape.373), calls=%async_computation.3 | async-start | bytes 262144 | tf_op jit(solution)/shard_map/all_to_all | solution.py:125
  275.6 338.4 %all-reduce.2.cloned.1.call-start = ((), (), s32[]{:S(2)}) async-start(), calls=%async_computation.6 | async-start | bytes 262144 | tf_op jit(solution)/shard_map/psum | solution.py:168
  296.6 5.1 copy-start.2
  316.3 8.3 %collective-permute-start.5 = (f32[2,2,32,512]{3,1,0,2:T(2,128)S(1)}, f32[2,2,32,512]{3,1,0,2:T(2,128)S(1)}, u32[]{:S(2)}, u32[]{:S(2)}) collective-permute-start(f32[2,2,32,512]{3,1,0,2:T(2,128)S(1)} %slice.75), channel_id=1, source_target_pairs={{480,0},{0,32},{32,64},{64,96},{96,128},{128,160},{160,192},{192,2... | collective-permute-start | bytes 786440 | tf_op jit(solution)/shard_map/ppermute | solution.py:13
  325.0 13.3 %collective-permute-start.6 = (f32[2,2,2,32,512]{4,2,0,3,1:T(2,128)S(1)}, f32[2,2,2,32,512]{4,2,0,3,1:T(2,128)S(1)}, u32[]{:S(2)}, u32[]{:S(2)}) collective-permute-start(f32[2,2,2,32,512]{4,2,0,3,1:T(2,128)S(1)} %pad_maximum_fusion), channel_id=1, source_target_pairs={{480,0},{0,32},{32,64},{64,96},{96,128},{128,160},{160,192},{192,2... | collective-permute-start | bytes 1572872 | tf_op jit(solution)/shard_map/ppermute | solution.py:13
  338.8 22.4 %collective-permute-start.7 = (f32[2,2,2,32,512]{4,2,0,3,1:T(2,128)S(1)}, f32[2,2,2,32,512]{4,2,0,3,1:T(2,128)S(1)}, u32[]{:S(2)}, u32[]{:S(2)}) collective-permute-start(f32[2,2,2,32,512]{4,2,0,3,1:T(2,128)S(1)} %broadcast_select_fusion), channel_id=1, source_target_pairs={{448,0},{480,32},{0,64},{32,96},{64,128},{96,160},{128,192},{160,2... | collective-permute-start | bytes 1572872 | tf_op jit(solution)/shard_map/ppermute | solution.py:13
  361.6 25.0 %collective-permute-start.8 = (f32[2,2,2,32,512]{4,2,0,3,1:T(2,128)S(1)}, f32[2,2,2,32,512]{4,2,0,3,1:T(2,128)S(1)}, u32[]{:S(2)}, u32[]{:S(2)}) collective-permute-start(f32[2,2,2,32,512]{4,2,0,3,1:T(2,128)S(1)} %broadcast_select_fusion.1), channel_id=1, source_target_pairs={{384,0},{416,32},{448,64},{480,96},{0,128},{32,160},{64,192},{96,2... | collective-permute-start | bytes 1572872 | tf_op jit(solution)/shard_map/ppermute | solution.py:13
  387.0 12.6 %collective-permute-start.9 = (f32[2,2,2,32,512]{4,2,0,3,1:T(2,128)S(1)}, f32[2,2,2,32,512]{4,2,0,3,1:T(2,128)S(1)}, u32[]{:S(2)}, u32[]{:S(2)}) collective-permute-start(f32[2,2,2,32,512]{4,2,0,3,1:T(2,128)S(1)} %broadcast_select_fusion.2), channel_id=1, source_target_pairs={{256,0},{288,32},{320,64},{352,96},{384,128},{416,160},{448,192},{... | collective-permute-start | bytes 1572872 | tf_op jit(solution)/shard_map/ppermute | solution.py:13
  397.2 342.6 %reduce-scatter.4.cloned.1.call-start = ((), (), s32[]{:S(2)}) async-start(), calls=%async_computation.7 | async-start | bytes 2162688
  399.9 0.8 copy-start.1
Sparse Core Ops, SparseCore 0:
  10.7 74.1 all-gather.1
  397.4 216.6 all-reduce.1
  616.8 122.9 reduce-scatter.3
where the time goes:
time: 754 us; the launch traced here: 749 us
  waiting for transfers between devices  474 us (63%)
  local copies, waits for them, and re-layouts  79.3 us (11%)
  matrix products  78 us (10%)
  starting transfers between devices  72.2 us (10%)
  other arithmetic  23.6 us (3%)
  between operations  21.3 us (3%)
    psum x1, waiting for transfers between devices, on_device(): probe_grad = lax.psum(probe_sum, 'scan')  169 us
    unnamed x4, waiting for transfers between devices  124 us
    ppermute x10, waiting for transfers between devices, from_behind(): return lax.ppermute(block, axis, route)  98.4 us
    dot_general x16, matrix products, contract(): jnp.einsum(form, left_side, right_side, precision=lax.Precision.HIGHEST,...  78 us
    all_gather x1, waiting for transfers between devices, on_device(): band_rows = lax.all_gather(object_slice, 'scan', axis=3, tiled=True)  73 us
    ppermute x10, starting transfers between devices, from_behind(): return lax.ppermute(block, axis, route)  41.7 us
    unnamed x26, local copies, waits for them, and re-layouts  26.5 us
    dynamic_update_slice x4, local copies, waits for them, and re-layouts, add_tile(): return lax.dynamic_update_slice(band_now, current + tile_value, corner)  24.7 us
  transfers between devices with their start and end apart: 17, of which 16 were waited for; matrix products, arithmetic and copies ran while one was open for 11% of the time, Pallas kernels for 0%

commit v1 on v0

--- a/solution.py
+++ b/solution.py
@@ -3,6 +3,7 @@
 import jax.numpy as jnp
 from jax import lax
 from jax.sharding import PartitionSpec as P
+from jax.lax import all_gather
 
 fresnel_scale = 4
 
@@ -46,6 +47,10 @@
 
 
 def on_device(object_slice, probe_field, offsets, assignment, intensities):
+
+    def record_obtain(buf, link_axis):
+        return jnp.sum(all_gather(buf, link_axis), 0)
+
     depth_count = lax.axis_size("depth")
     depth_index = lax.axis_index("depth")
     rows_dev = object_slice.shape[2]
@@ -165,7 +170,7 @@
             grad_band, grad_pair[slot_index, 1], second_cycle[slot_index], left_col[slot_index]
         )
     probe_sum = jnp.stack([jnp.sum(term_re, 0), jnp.sum(term_im, 0)])
-    probe_grad = lax.psum(probe_sum, "scan")
+    probe_grad = record_obtain(probe_sum, "scan")
     object_grad = lax.psum_scatter(
         grad_band.reshape(2, cycles, rows_dev, full_width), "scan", scatter_dimension=3, tiled=True
     )

time: 754 us -> 658 us (0.87)
  the two profiles are of different devices: /device:TPU:8 before, /device:TPU:1 now
where the time goes in v1:
time: 658 us; the launch traced here: 653 us
  waiting for transfers between devices  384 us (58%)
  local copies, waits for them, and re-layouts  79.2 us (12%)
  matrix products  78 us (12%)
  starting transfers between devices  64.2 us (10%)
  other arithmetic  25.2 us (4%)
  between operations  21.3 us (3%)
    unnamed x4, waiting for transfers between devices  120 us
    ppermute x10, waiting for transfers between devices, from_behind(): return lax.ppermute(block, axis, route)  111 us
    dot_general x16, matrix products, contract(): jnp.einsum(form, left_side, right_side, precision=lax.Precision.HIGHEST,...  78 us
    all_gather x1, waiting for transfers between devices, on_device(): band_rows = lax.all_gather(object_slice, 'scan', axis=3, tiled=True)  74.3 us
    all_gather x1, waiting for transfers between devices, record_obtain(): return jnp.sum(all_gather(buf, link_axis), 0)  71.9 us
    ppermute x10, starting transfers between devices, from_behind(): return lax.ppermute(block, axis, route)  36.6 us
    unnamed x26, local copies, waits for them, and re-layouts  26.5 us
    dynamic_update_slice x4, local copies, waits for them, and re-layouts, add_tile(): return lax.dynamic_update_slice(band_now, current + tile_value, corner)  24.6 us
  transfers between devices with their start and end apart: 17, of which 16 were waited for; matrix products, arithmetic and copies ran while one was open for 6% of the time, Pallas kernels for 0%

profile of v1, /device:TPU:1, one launch (start us, length us, event | category | flops | bytes accessed | tf_op | source)
XLA Modules:
  0.0 652.7 jit_solution(10508709182147924221)
XLA Ops:
  7.2 1.7 copy.63
  11.9 74.3 %all-gather.4.cloned.1.call-done = bf16[2,4,32,2048]{2,1,0,3:T(4,128)(2,1)} async-done(((bf16[2,4,32,64]{2,1,0,3:T(4,128)(2,1)}), bf16[2,4,32,2048]{2,1,0,3:T(4,128)(2,1)}) %all-gather.4.cloned.1.call-update) | async-done | bytes 1048592 | tf_op jit(solution)/shard_map/all_gather | solution.py:61
  86.2 5.5 copy.64
  91.8 4.2 while.4
  92.5 1.4 dynamic-slice_bitcast_fusion.6
  94.6 1.4 dynamic-slice_bitcast_fusion.6
  96.1 4.2 while.3
  96.7 1.4 dynamic-slice_bitcast_fusion.5
  98.8 1.4 dynamic-slice_bitcast_fusion.5
  100.7 3.1 collective-permute-start
  103.9 9.9 %collective-permute-done = bf16[2,2,2,32,512]{4,2,0,3,1:T(2,128)(2,1)S(1)} collective-permute-done((bf16[2,2,2,32,512]{4,2,0,3,1:T(2,128)(2,1)S(1)}, bf16[2,2,2,32,512]{4,2,0,3,1:T(2,128)(2,1)S(1)}, u32[]{:S(2)}, u32[]{:S(2)}) %collective-permute-start) | collective-permute-done | bytes 262176 | tf_op jit(solution)/shard_map/ppermute | solution.py:14
  114.3 1.9 collective-permute-start.1
  116.3 16.1 %collective-permute-done.1 = bf16[2,2,2,32,512]{4,2,0,3,1:T(2,128)(2,1)S(1)} collective-permute-done((bf16[2,2,2,32,512]{4,2,0,3,1:T(2,128)(2,1)S(1)}, bf16[2,2,2,32,512]{4,2,0,3,1:T(2,128)(2,1)S(1)}, u32[]{:S(2)}, u32[]{:S(2)}) %collective-permute-start.1) | collective-permute-done | bytes 262176 | tf_op jit(solution)/shard_map/ppermute | solution.py:14
  133.0 2.1 collective-permute-start.2
  135.2 17.0 %collective-permute-done.2 = bf16[2,2,2,32,512]{4,2,0,3,1:T(2,128)(2,1)S(1)} collective-permute-done((bf16[2,2,2,32,512]{4,2,0,3,1:T(2,128)(2,1)S(1)}, bf16[2,2,2,32,512]{4,2,0,3,1:T(2,128)(2,1)S(1)}, u32[]{:S(2)}, u32[]{:S(2)}) %collective-permute-start.2) | collective-permute-done | bytes 262176 | tf_op jit(solution)/shard_map/ppermute | solution.py:14
  152.6 1.9 collective-permute-start.3
  154.6 8.4 %collective-permute-done.3 = bf16[2,2,2,32,512]{4,2,0,3,1:T(2,128)(2,1)S(1)} collective-permute-done((bf16[2,2,2,32,512]{4,2,0,3,1:T(2,128)(2,1)S(1)}, bf16[2,2,2,32,512]{4,2,0,3,1:T(2,128)(2,1)S(1)}, u32[]{:S(2)}, u32[]{:S(2)}) %collective-permute-start.3) | collective-permute-done | bytes 262176 | tf_op jit(solution)/shard_map/ppermute | solution.py:14
  163.5 2.1 collective-permute-start.4
  165.7 3.5 collective-permute-done.4
  170.6 5.0 fusion.27
  175.6 5.0 fusion.23
  180.6 5.2 fusion.1
  187.3 5.0 all-to-all-start
  192.3 5.0 fusion
  198.8 2.5 all-to-all-done
  201.2 7.0 %all-to-all-start.1 = ((f32[16,1,2048]{2,1,0:T(1,128)}), f32[16,1,2048]{2,1,0:T(1,128)S(1)}, u32[]{:S(2)}, u32[]{:S(2)}) async-start(f32[16,1,2048]{2,1,0:T(1,128)} %reshape.372), calls=%async_computation.1 | async-start | bytes 262144 | tf_op jit(solution)/shard_map/all_to_all | solution.py:121
  210.7 4.8 fusion.25
  215.5 4.8 fusion.10
  222.2 4.7 convolution_add_fusion.2
  227.0 5.0 convolution_subtract_fusion.2
  231.9 4.8 fusion.7
  236.8 4.8 fusion.20
  241.6 4.8 convolution_subtract_fusion.1
  247.8 9.2 %all-to-all-start.2 = ((f32[16,1,2048]{2,1,0:T(1,128)}), f32[16,1,2048]{2,1,0:T(1,128)S(1)}, u32[]{:S(2)}, u32[]{:S(2)}) async-start(f32[16,1,2048]{2,1,0:T(1,128)} %reshape.376), calls=%async_computation.2 | async-start | bytes 262144 | tf_op jit(solution)/shard_map/all_to_all | solution.py:129
  257.0 4.8 convolution_add_fusion.1
  263.2 2.7 all-to-all-done.2
  265.9 6.3 all-to-all-start.3
  274.3 5.0 fusion.18
  279.3 1.9 all-to-all-done.3
  283.1 4.8 fusion.15
  287.9 4.8 convolution_add_fusion
  292.7 4.9 fusion.40
  297.8 14.5 %while.5 = (s32[]{:T(128)}, f32[2,2,64,512]{3,1,0,2:T(2,128)S(1)}, s32[2,4]{1,0:T(2,128)S(1)}, f32[2,2,32,512]{3,2,0,1:T(8,128)S(1)}, s32[]{:T(128)}, /*index=5*/s32[4]{0:T(128)S(1)}) while((s32[]{:T(128)}, f32[2,2,64,512]{3,1,0,2:T(2,128)S(1)}, s32[2,4]{1,0:T(2,128)S(1)}, f32[2,2,32,512]{3,2,0,1:T(8,128)S(1)}, s32[]{:T(128)}, ...), condition=%wide.while_cond.2, body=%wide.while_body.2.sunk | while | flops 32797 | bytes 917703 | solution.py:150
  298.5 3.2 and_reduce_fusion.2
  305.7 3.2 and_reduce_fusion.2
  312.3 3.0 collective-permute-start.5
  315.3 7.7 %collective-permute-done.5 = f32[2,2,32,512]{3,1,0,2:T(2,128)S(1)} collective-permute-done((f32[2,2,32,512]{3,1,0,2:T(2,128)S(1)}, f32[2,2,32,512]{3,1,0,2:T(2,128)S(1)}, u32[]{:S(2)}, u32[]{:S(2)}) %collective-permute-start.5) | collective-permute-done | bytes 262176 | tf_op jit(solution)/shard_map/ppermute | solution.py:14
  323.5 2.2 collective-permute-start.6
  325.7 11.4 %collective-permute-done.6 = f32[2,2,2,32,512]{4,2,0,3,1:T(2,128)S(1)} collective-permute-done((f32[2,2,2,32,512]{4,2,0,3,1:T(2,128)S(1)}, f32[2,2,2,32,512]{4,2,0,3,1:T(2,128)S(1)}, u32[]{:S(2)}, u32[]{:S(2)}) %collective-permute-start.6) | collective-permute-done | bytes 524320 | tf_op jit(solution)/shard_map/ppermute | solution.py:14
  337.4 1.9 collective-permute-start.7
  339.4 16.0 %collective-permute-done.7 = f32[2,2,2,32,512]{4,2,0,3,1:T(2,128)S(1)} collective-permute-done((f32[2,2,2,32,512]{4,2,0,3,1:T(2,128)S(1)}, f32[2,2,2,32,512]{4,2,0,3,1:T(2,128)S(1)}, u32[]{:S(2)}, u32[]{:S(2)}) %collective-permute-start.7) | collective-permute-done | bytes 524320 | tf_op jit(solution)/shard_map/ppermute | solution.py:14
  355.9 4.2 collective-permute-start.8
  360.0 17.5 %collective-permute-done.8 = f32[2,2,2,32,512]{4,2,0,3,1:T(2,128)S(1)} collective-permute-done((f32[2,2,2,32,512]{4,2,0,3,1:T(2,128)S(1)}, f32[2,2,2,32,512]{4,2,0,3,1:T(2,128)S(1)}, u32[]{:S(2)}, u32[]{:S(2)}) %collective-permute-start.8) | collective-permute-done | bytes 524320 | tf_op jit(solution)/shard_map/ppermute | solution.py:14
  377.9 14.2 %collective-permute-start.9 = (f32[2,2,2,32,512]{4,2,0,3,1:T(2,128)S(1)}, f32[2,2,2,32,512]{4,2,0,3,1:T(2,128)S(1)}, u32[]{:S(2)}, u32[]{:S(2)}) collective-permute-start(f32[2,2,2,32,512]{4,2,0,3,1:T(2,128)S(1)} %broadcast_select_fusion.2), channel_id=1, source_target_pairs={{256,0},{288,32},{320,64},{352,96},{384,128},{416,160},{448,192},{... | collective-permute-start | bytes 1572872 | tf_op jit(solution)/shard_map/ppermute | solution.py:14
  399.7 3.8 collective-permute-done.9
  405.7 6.1 dynamic_update_slice.12
  413.0 6.1 dynamic_update_slice.13
  420.3 6.1 dynamic_update_slice.14
  427.6 6.1 dynamic_update_slice.15
  433.7 6.1 copy.84
  439.8 8.6 %reshape.366 = f32[2048,256]{1,0:T(8,128)} reshape(f32[2048,2,4,32]{3,2,1,0:T(4,128)} %bitcast.196) | data formatting | bytes 4194304
  449.2 119.7 %reduce-scatter.4.cloned.1.call-done = f32[64,256]{1,0:T(8,128)} async-done(((f32[2048,256]{1,0:T(8,128)}), f32[64,256]{1,0:T(8,128)}) %reduce-scatter.4.cloned.1.call-update) | async-done | bytes 65552
  570.7 71.9 %all-gather.6.cloned.1.call-done = f32[64,32,512]{2,1,0:T(8,128)} async-done(((f32[2,32,512]{2,1,0:T(8,128)}), f32[64,32,512]{2,1,0:T(8,128)}) %all-gather.6.cloned.1.call-update) | async-done | bytes 4194320 | tf_op jit(solution)/shard_map/all_gather | solution.py:52
  642.6 2.5 reduce_sum.29
  (116 shorter events, 43.6 us)
Async XLA Ops:
  7.2 109.1 %copy-start = (bf16[2,512,512]{2,1,0:T(8,128)(2,1)S(1)}, bf16[2,512,512]{2,1,0:T(8,128)(2,1)}, u32[]{:S(2)}) copy-start(bf16[2,512,512]{2,1,0:T(8,128)(2,1)} %param.6) | copy-start | bytes 3145732
  7.2 79.1 %all-gather.4.cloned.1.call-start = ((), (), s32[]{:S(2)}) async-start(), calls=%async_computation.5 | async-start | bytes 4325376 | tf_op jit(solution)/shard_map/all_gather | solution.py:61
  100.7 13.1 %collective-permute-start = (bf16[2,2,2,32,512]{4,2,0,3,1:T(2,128)(2,1)S(1)}, bf16[2,2,2,32,512]{4,2,0,3,1:T(2,128)(2,1)S(1)}, u32[]{:S(2)}, u32[]{:S(2)}) collective-permute-start(bf16[2,2,2,32,512]{4,2,0,3,1:T(2,128)(2,1)S(1)} %pad_maximum_fusion.1), channel_id=1, source_target_pairs={{480,0},{0,32},{32,64},{64,96},{96,128},{128,160},{160,192},{192,2... | collective-permute-start | bytes 786440 | tf_op jit(solution)/shard_map/ppermute | solution.py:14
  114.3 18.1 %collective-permute-start.1 = (bf16[2,2,2,32,512]{4,2,0,3,1:T(2,128)(2,1)S(1)}, bf16[2,2,2,32,512]{4,2,0,3,1:T(2,128)(2,1)S(1)}, u32[]{:S(2)}, u32[]{:S(2)}) collective-permute-start(bf16[2,2,2,32,512]{4,2,0,3,1:T(2,128)(2,1)S(1)} %broadcast_select_fusion.4), channel_id=1, source_target_pairs={{448,0},{480,32},{0,64},{32,96},{64,128},{96,160},{128,192},{160,2... | collective-permute-start | bytes 786440 | tf_op jit(solution)/shard_map/ppermute | solution.py:14
  133.0 19.3 %collective-permute-start.2 = (bf16[2,2,2,32,512]{4,2,0,3,1:T(2,128)(2,1)S(1)}, bf16[2,2,2,32,512]{4,2,0,3,1:T(2,128)(2,1)S(1)}, u32[]{:S(2)}, u32[]{:S(2)}) collective-permute-start(bf16[2,2,2,32,512]{4,2,0,3,1:T(2,128)(2,1)S(1)} %broadcast_select_fusion.5), channel_id=1, source_target_pairs={{384,0},{416,32},{448,64},{480,96},{0,128},{32,160},{64,192},{96,2... | collective-permute-start | bytes 786440 | tf_op jit(solution)/shard_map/ppermute | solution.py:14
  152.6 10.4 %collective-permute-start.3 = (bf16[2,2,2,32,512]{4,2,0,3,1:T(2,128)(2,1)S(1)}, bf16[2,2,2,32,512]{4,2,0,3,1:T(2,128)(2,1)S(1)}, u32[]{:S(2)}, u32[]{:S(2)}) collective-permute-start(bf16[2,2,2,32,512]{4,2,0,3,1:T(2,128)(2,1)S(1)} %broadcast_select_fusion.6), channel_id=1, source_target_pairs={{256,0},{288,32},{320,64},{352,96},{384,128},{416,160},{448,192},{... | collective-permute-start | bytes 786440 | tf_op jit(solution)/shard_map/ppermute | solution.py:14
  163.5 5.7 collective-permute-start.4
  187.3 13.9 %all-to-all-start = ((f32[16,1,2048]{2,1,0:T(1,128)}), f32[16,1,2048]{2,1,0:T(1,128)S(1)}, u32[]{:S(2)}, u32[]{:S(2)}) async-start(f32[16,1,2048]{2,1,0:T(1,128)} %reshape.370), calls=%async_computation | async-start | bytes 262144 | tf_op jit(solution)/shard_map/all_to_all | solution.py:120
  201.2 19.0 %all-to-all-start.1 = ((f32[16,1,2048]{2,1,0:T(1,128)}), f32[16,1,2048]{2,1,0:T(1,128)S(1)}, u32[]{:S(2)}, u32[]{:S(2)}) async-start(f32[16,1,2048]{2,1,0:T(1,128)} %reshape.372), calls=%async_computation.1 | async-start | bytes 262144 | tf_op jit(solution)/shard_map/all_to_all | solution.py:121
  227.0 5.0 copy-start.3
  247.8 18.1 %all-to-all-start.2 = ((f32[16,1,2048]{2,1,0:T(1,128)}), f32[16,1,2048]{2,1,0:T(1,128)S(1)}, u32[]{:S(2)}, u32[]{:S(2)}) async-start(f32[16,1,2048]{2,1,0:T(1,128)} %reshape.376), calls=%async_computation.2 | async-start | bytes 262144 | tf_op jit(solution)/shard_map/all_to_all | solution.py:129
  265.9 15.3 %all-to-all-start.3 = ((f32[16,1,2048]{2,1,0:T(1,128)}), f32[16,1,2048]{2,1,0:T(1,128)S(1)}, u32[]{:S(2)}, u32[]{:S(2)}) async-start(f32[16,1,2048]{2,1,0:T(1,128)} %reshape.374), calls=%async_computation.3 | async-start | bytes 262144 | tf_op jit(solution)/shard_map/all_to_all | solution.py:130
  272.2 296.6 %reduce-scatter.4.cloned.1.call-start = ((), (), s32[]{:S(2)}) async-start(), calls=%async_computation.7 | async-start | bytes 2162688
  292.7 5.2 copy-start.2
  312.3 10.7 %collective-permute-start.5 = (f32[2,2,32,512]{3,1,0,2:T(2,128)S(1)}, f32[2,2,32,512]{3,1,0,2:T(2,128)S(1)}, u32[]{:S(2)}, u32[]{:S(2)}) collective-permute-start(f32[2,2,32,512]{3,1,0,2:T(2,128)S(1)} %slice.75), channel_id=1, source_target_pairs={{480,0},{0,32},{32,64},{64,96},{96,128},{128,160},{160,192},{192,2... | collective-permute-start | bytes 786440 | tf_op jit(solution)/shard_map/ppermute | solution.py:14
  323.5 13.5 %collective-permute-start.6 = (f32[2,2,2,32,512]{4,2,0,3,1:T(2,128)S(1)}, f32[2,2,2,32,512]{4,2,0,3,1:T(2,128)S(1)}, u32[]{:S(2)}, u32[]{:S(2)}) collective-permute-start(f32[2,2,2,32,512]{4,2,0,3,1:T(2,128)S(1)} %pad_maximum_fusion), channel_id=1, source_target_pairs={{480,0},{0,32},{32,64},{64,96},{96,128},{128,160},{160,192},{192,2... | collective-permute-start | bytes 1572872 | tf_op jit(solution)/shard_map/ppermute | solution.py:14
  337.4 17.9 %collective-permute-start.7 = (f32[2,2,2,32,512]{4,2,0,3,1:T(2,128)S(1)}, f32[2,2,2,32,512]{4,2,0,3,1:T(2,128)S(1)}, u32[]{:S(2)}, u32[]{:S(2)}) collective-permute-start(f32[2,2,2,32,512]{4,2,0,3,1:T(2,128)S(1)} %broadcast_select_fusion), channel_id=1, source_target_pairs={{448,0},{480,32},{0,64},{32,96},{64,128},{96,160},{128,192},{160,2... | collective-permute-start | bytes 1572872 | tf_op jit(solution)/shard_map/ppermute | solution.py:14
  355.9 21.7 %collective-permute-start.8 = (f32[2,2,2,32,512]{4,2,0,3,1:T(2,128)S(1)}, f32[2,2,2,32,512]{4,2,0,3,1:T(2,128)S(1)}, u32[]{:S(2)}, u32[]{:S(2)}) collective-permute-start(f32[2,2,2,32,512]{4,2,0,3,1:T(2,128)S(1)} %broadcast_select_fusion.1), channel_id=1, source_target_pairs={{384,0},{416,32},{448,64},{480,96},{0,128},{32,160},{64,192},{96,2... | collective-permute-start | bytes 1572872 | tf_op jit(solution)/shard_map/ppermute | solution.py:14
  377.9 25.6 %collective-permute-start.9 = (f32[2,2,2,32,512]{4,2,0,3,1:T(2,128)S(1)}, f32[2,2,2,32,512]{4,2,0,3,1:T(2,128)S(1)}, u32[]{:S(2)}, u32[]{:S(2)}) collective-permute-start(f32[2,2,2,32,512]{4,2,0,3,1:T(2,128)S(1)} %broadcast_select_fusion.2), channel_id=1, source_target_pairs={{256,0},{288,32},{320,64},{352,96},{384,128},{416,160},{448,192},{... | collective-permute-start | bytes 1572872 | tf_op jit(solution)/shard_map/ppermute | solution.py:14
  403.9 0.8 copy-start.1
  448.4 194.1 %all-gather.6.cloned.1.call-start = ((), (), s32[]{:S(2)}) async-start(), calls=%async_computation.6 | async-start | bytes 4325376 | tf_op jit(solution)/shard_map/all_gather | solution.py:52
Sparse Core Ops, SparseCore 0:
  10.7 75.4 all-gather.3
  448.5 120.2 reduce-scatter.3
  571.6 70.9 all-gather.5
